TPU v7x, 32 devices: a whole 2x2x4 slice. The times are simulated.
32 devices in a mesh: ep: 16 (over z, y, core), dp: 2 (over x).
Axes of the slice: x: 2, y: 2, z: 4, core: 2. Of those that a mesh axis runs over, the one named last changes fastest.
Arguments:
- moe_rows: bfloat16 [1024, 3584], P(('dp', 'ep')), parts along dimension 0, may hold values from -6 to 6
- routes: int32 [1024, 4], P(('dp', 'ep')), parts along dimension 0, may hold values from 0 to 7, all different within a row; in each aligned block of 32 rows (0 to 31, 32 to 63, ...) at most 32 rows name the same one
- route_weights: float32 [1024, 4], P(('dp', 'ep')), parts along dimension 0, may hold values from 0.05 to 0.5
- w_gate: bfloat16 [16, 3584, 512], P('ep'), may hold values from -0.09375 to 0.09375
- w_up: bfloat16 [16, 3584, 512], P('ep'), may hold values from -0.09375 to 0.09375
- w_down: bfloat16 [16, 512, 3584], P('ep'), may hold values from -0.1875 to 0.1875
- queries: bfloat16 [128, 64, 576], P(('dp', 'ep')), parts along dimension 0, may hold values from -45 to 45
- latent_cache: bfloat16 [128, 128, 576], P(('dp', 'ep')), parts along dimension 0, may hold values from -6 to 6
- lengths: int32 [128], P(('dp', 'ep')), parts along dimension 0, may hold values from 2 to 128, as said below
Outputs:
- moe_out: bfloat16 [1024, 3584], P(('dp', 'ep')), parts along dimension 0
- attn_out: bfloat16 [128, 64, 512], P(('dp', 'ep')), parts along dimension 0
There are 2 independent parts, one for each index of `dp`. A program takes and returns all parts, laid end to end along the dimension named above; an argument that names none is the same for every part. Nothing has to cross between parts.
Inputs may be any that keep to these rules, and one draw needn't show every extreme that they name: `routes`: each row names 4 different experts; in each aligned block of 32 rows (the rows of one device) no expert is named by more than 32 rows, a bound that some block reaches. `lengths`: some row of every part uses all 128 positions.
All inputs are finite; a program needn't handle non-finite values.
Results may differ from a plain program's by a relative error of at most 0.0085.
Values may be sent and summed in bfloat16 or wider, within the bound.
No kernel may reach another device: no remote copies, remote signals or barrier semaphores. Data moves between devices by JAX's collectives and lax.ppermute only.
A program may use at most 128 MiB of HBM per device.

v0:
```python
import jax
import jax.numpy as jnp
from jax import lax
from jax.sharding import PartitionSpec as P

LATENT = 512
score_scale = 192.0 ** (-0.5)


def attend(queries, latent_cache, lengths):
    scores = (
        jnp.einsum("rhc,rlc->rhl", queries, latent_cache, preferred_element_type=jnp.float32)
        * score_scale
    )
    in_range = (
        jnp.arange(latent_cache.shape[1], dtype=jnp.int32)[None, None, :] < lengths[:, None, None]
    )
    scores = jnp.where(in_range, scores, -1e30)
    highest = jnp.max(scores, axis=-1, keepdims=True)
    expo = jnp.where(in_range, jnp.exp(scores - highest), 0.0)
    probs = (expo / jnp.sum(expo, axis=-1, keepdims=True)).astype(jnp.bfloat16)
    return jnp.einsum(
        "rhl,rlc->rhc", probs, latent_cache[:, :, :LATENT], preferred_element_type=jnp.float32
    ).astype(jnp.bfloat16)


def shards(moe_rows, routes, route_weights, w_gate, w_up, w_down, queries, latent_cache, lengths):
    attn_out = attend(queries, latent_cache, lengths)
    rows_here, model_width = moe_rows.shape
    experts = lax.axis_size("ep") // 2
    expert = lax.axis_index("ep") // 2
    named = routes[:, :, None] == jnp.arange(experts, dtype=jnp.int32)[None, None, :]
    dense_w = jnp.sum(jnp.where(named, route_weights[:, :, None], 0.0), axis=1)
    hi = dense_w.astype(jnp.bfloat16)
    rest = dense_w - hi.astype(jnp.float32)
    mid = rest.astype(jnp.bfloat16)
    lo = (rest - mid.astype(jnp.float32)).astype(jnp.bfloat16)
    extra = -(-3 * experts // 128) * 128
    tail = jnp.zeros((rows_here, extra - 3 * experts), jnp.bfloat16)
    packed = jnp.concatenate([moe_rows, hi, mid, lo, tail], axis=1)
    gathered = lax.all_gather(packed, "ep", axis=0, tiled=True)
    all_rows = gathered[:, :model_width]
    parts = gathered[:, model_width : model_width + 3 * experts].astype(jnp.float32)
    parts = parts.reshape(-1, 3, experts)
    weight_all = parts[:, 0] + (parts[:, 1] + parts[:, 2])
    weight = jnp.sum(jnp.where(jnp.arange(experts)[None, :] == expert, weight_all, 0.0), axis=1)
    gate_act = jnp.dot(all_rows, w_gate[0], preferred_element_type=jnp.float32)
    up_act = jnp.dot(all_rows, w_up[0], preferred_element_type=jnp.float32)
    hidden = (jax.nn.silu(gate_act) * up_act).astype(jnp.bfloat16)
    partial_out = jnp.dot(hidden, w_down[0], preferred_element_type=jnp.float32)
    partial_out = partial_out * weight[:, None]
    moe_out = lax.psum_scatter(partial_out, "ep", scatter_dimension=0, tiled=True)
    return (moe_out.astype(jnp.bfloat16), attn_out)


def solution(mesh):
    in_specs = (
        P(("dp", "ep"), None),
        P(("dp", "ep"), None),
        P(("dp", "ep"), None),
        P("ep", None, None),
        P("ep", None, None),
        P("ep", None, None),
        P(("dp", "ep"), None, None),
        P(("dp", "ep"), None, None),
        P(("dp", "ep")),
    )
    out_specs = (P(("dp", "ep"), None), P(("dp", "ep"), None, None))
    return jax.shard_map(shards, mesh=mesh, in_specs=in_specs, out_specs=out_specs, check_vma=False)
```

profile of v0, /device:TPU:0, one launch (start us, length us, event | category | flops | bytes accessed | tf_op | source)
XLA Modules:
  0.0 178.8 jit_solution(15685329627394911693)
XLA Ops:
  7.2 0.0 copy-start
  7.2 0.0 all-gather.2.cloned.1.call-start
  7.2 0.7 select_reduce_fusion
  8.0 0.1 copy.22
  8.1 0.1 copy.23
  8.2 0.1 copy.24
  8.3 1.7 concatenate.3
  10.0 0.0 all-gather.2.cloned.1.call-update
  10.0 0.0 reduce-scatter.2.cloned.1.call-start
  10.1 51.7 %all-gather.2.cloned.1.call-done = bf16[512,3712]{1,0:T(8,128)(2,1)} async-done(((bf16[32,3712]{1,0:T(8,128)(2,1)}), bf16[512,3712]{1,0:T(8,128)(2,1)}) %all-gather.2.cloned.1.call-update) | async-done | bytes 3801104 | tf_op jit(solution)/shard_map/all_gather | solution.py:41
  61.7 0.9 slice.25
  62.6 0.1 copy.27
  62.7 0.1 fusion.32
  62.8 5.2 %fusion.4 = f32[512,512]{1,0:T(8,128)S(1)} fusion(bf16[1,3584,512]{2,1,0:T(8,128)(2,1)} %param.12, bf16[512,3712]{1,0:T(8,128)(2,1)} %all-gather.2.cloned.1.call-done), kind=kOutput, calls=%fused_computation.5 | convolution fusion | flops 1879048192 | bytes 8388608 | tf_op jit(solution)/shard_map/dot_general | solution.py:47
  68.0 11.2 %convolution_multiply_fusion = f32[512,3584]{1,0:T(8,128)} fusion(bf16[1,512,3584]{2,1,0:T(8,128)(2,1)} %param.14, f32[512]{0:T(512)S(1)} %fusion.32, bf16[1,3584,512]{2,1,0:T(8,128)(2,1)} %param.13, bf16[512,3712]{1,0:T(8,128)(2,1)} %all-gather.2.cloned.1.call-done, f32[512,512]{1,0:T(8,128)S(1)} %fusion.4), kind=kOutput, calls=%fused_computation.1 | convolution fusion | flops 3761504256 | bytes 19400704 | tf_op jit(solution)/shard_map/dot_general | solution.py:50
  79.3 0.0 reduce-scatter.2.cloned.1.call-update
  79.3 0.6 copy-done.2
  79.9 0.1 iota_compare_fusion.1
  80.0 0.3 copy-done.1
  80.3 0.2 fusion.19
  80.6 0.2 fusion.37
  80.8 1.3 convolution_convert_fusion
  82.1 88.2 %reduce-scatter.2.cloned.1.call-done = f32[32,3584]{1,0:T(8,128)} async-done(((f32[512,3584]{1,0:T(8,128)}), f32[32,3584]{1,0:T(8,128)}) %reduce-scatter.2.cloned.1.call-update) | async-done | bytes 458768 | tf_op jit(solution)/shard_map/reduce_scatter | solution.py:52
  170.2 1.7 convert_element_type.34
  (7 shorter events, 0.0 us)
Async XLA Ops:
  7.2 72.8 %copy-start = (bf16[4,64,576]{2,1,0:T(8,128)(2,1)S(1)}, bf16[4,64,576]{2,1,0:T(8,128)(2,1)}, u32[]{:S(2)}) copy-start(bf16[4,64,576]{2,1,0:T(8,128)(2,1)} %param.15) | copy-start | bytes 884740
  7.2 54.6 %all-gather.2.cloned.1.call-start = ((), (), s32[]{:S(2)}) async-start(), calls=%async_computation.1 | async-start | bytes 4038656 | tf_op jit(solution)/shard_map/all_gather | solution.py:41
  10.0 160.2 %reduce-scatter.2.cloned.1.call-start = ((), (), s32[]{:S(2)}) async-start(), calls=%async_computation.2 | async-start | bytes 7798784 | tf_op jit(solution)/shard_map/reduce_scatter | solution.py:52
  79.3 0.7 copy-start.2
  79.3 1.1 copy-start.1
Sparse Core Ops, SparseCore 0:
  10.9 50.8 all-gather.1
  79.4 90.7 reduce-scatter.1
where the time goes:
time: 179 us
  waiting for transfers between devices  140 us (78%)
  matrix products  18 us (10%)
  between operations  14.1 us (8%)
  local copies, waits for them, and re-layouts  3.97 us (2%)
  other arithmetic  2.85 us (2%)
    reduce_scatter x1, waiting for transfers between devices, shards(): lax.psum_scatter(partial_out, 'ep', scatter_dimension=0, tiled=True)  88.2 us
    all_gather x1, waiting for transfers between devices, shards(): gathered = lax.all_gather(packed, 'ep', axis=0, tiled=True)  51.7 us
    dot_general x1, matrix products, shards(): partial_out = jnp.dot(hidden, w_down[0], preferred_element_type=jnp.float32)  11.2 us
    dot_general x1, matrix products, shards(): gate_act = jnp.dot(all_rows, w_gate[0], preferred_element_type=jnp.float32)  5.21 us
  transfers between devices with their start and end apart: 2, of which 2 were waited for; matrix products, arithmetic and copies ran while one was open for 1% of the time, Pallas kernels for 0%

commit v1 on v0

--- a/solution.py
+++ b/solution.py
@@ -38,7 +38,12 @@
     extra = -(-3 * experts // 128) * 128
     tail = jnp.zeros((rows_here, extra - 3 * experts), jnp.bfloat16)
     packed = jnp.concatenate([moe_rows, hi, mid, lo, tail], axis=1)
-    gathered = lax.all_gather(packed, "ep", axis=0, tiled=True)
+    ring = [packed]
+    for hop in range(15):
+        ring.append(lax.ppermute(ring[-1], "ep", [(dev, (dev + 1) % 16) for dev in range(16)]))
+    gathered = jnp.roll(
+        jnp.concatenate(ring[::-1], axis=0), (lax.axis_index("ep") + 1) * ring[0].shape[0], axis=0
+    )
     all_rows = gathered[:, :model_width]
     parts = gathered[:, model_width : model_width + 3 * experts].astype(jnp.float32)
     parts = parts.reshape(-1, 3, experts)

time: 179 us -> 320 us (1.79); the launches traced: 179 us -> 316 us
  local copies, waits for them, and re-layouts: 3.97 us -> 70.4 us
  waiting for transfers between devices: 140 us -> 206 us
    ppermute x0 -> x15, waiting for transfers between devices: none -> 116 us  [shards(): lax.ppermute(ring[-1], 'ep', [(dev, (dev + 1) % 16) for dev in range(16)])]
    all_gather x1 -> x0, waiting for transfers between devices: 51.7 us -> none  [shards(): gathered = lax.all_gather(packed, 'ep', axis=0, tiled=True)]
    concatenate x0 -> x1, local copies, waits for them, and re-layouts: none -> 33.6 us  [shards(): jnp.roll(jnp.concatenate(ring[::-1], axis=0), (lax.axis_index('ep') + 1)...]
    ppermute x0 -> x15, local copies, waits for them, and re-layouts: none -> 28.3 us  [shards(): lax.ppermute(ring[-1], 'ep', [(dev, (dev + 1) % 16) for dev in range(16)])]
    unnamed x7 -> x34, local copies, waits for them, and re-layouts: 1.07 us -> 8.02 us
  transfers between devices with their start and end apart: 2 -> 16, of which waited for: 2 -> 15; matrix products, arithmetic and copies ran while one was open for 1% -> 9% of each run, Pallas kernels for 0% -> 0%
where the time goes in v1:
time: 320 us; the launch traced here: 316 us
  waiting for transfers between devices  206 us (64%)
  local copies, waits for them, and re-layouts  70.4 us (22%)
  matrix products  20.9 us (7%)
  between operations  14.1 us (4%)
  other arithmetic  3.68 us (1%)
    ppermute x15, waiting for transfers between devices, shards(): lax.ppermute(ring[-1], 'ep', [(dev, (dev + 1) % 16) for dev in range(16)])  116 us
    reduce_scatter x1, waiting for transfers between devices, shards(): lax.psum_scatter(partial_out, 'ep', scatter_dimension=0, tiled=True)  90.1 us
    concatenate x1, local copies, waits for them, and re-layouts, shards(): jnp.roll(jnp.concatenate(ring[::-1], axis=0), (lax.axis_index('ep') + 1)...  33.6 us
    ppermute x15, local copies, waits for them, and re-layouts, shards(): lax.ppermute(ring[-1], 'ep', [(dev, (dev + 1) % 16) for dev in range(16)])  28.3 us
    dot_general x1, matrix products, shards(): partial_out = jnp.dot(hidden, w_down[0], preferred_element_type=jnp.float32)  13.2 us
    unnamed x34, local copies, waits for them, and re-layouts  8.02 us
  transfers between devices with their start and end apart: 16, of which 15 were waited for; matrix products, arithmetic and copies ran while one was open for 9% of the time, Pallas kernels for 0%

profile of v1, /device:TPU:0, one launch (start us, length us, event | category | flops | bytes accessed | tf_op | source)
XLA Modules:
  0.0 315.6 jit_solution(5471722091449369583)
XLA Ops:
  10.3 8.8 %collective-permute-done = bf16[32,3712]{1,0:T(8,128)(2,1)S(1)} collective-permute-done((bf16[32,3712]{1,0:T(8,128)(2,1)S(1)}, bf16[32,3712]{1,0:T(8,128)(2,1)S(1)}, u32[]{:S(2)}, u32[]{:S(2)}) %collective-permute-start) | collective-permute-done | bytes 237600 | tf_op jit(solution)/shard_map/ppermute | solution.py:43
  19.1 8.2 %collective-permute-done.1 = bf16[32,3712]{1,0:T(8,128)(2,1)S(1)} collective-permute-done((bf16[32,3712]{1,0:T(8,128)(2,1)S(1)}, bf16[32,3712]{1,0:T(8,128)(2,1)S(1)}, u32[]{:S(2)}, u32[]{:S(2)}) %collective-permute-start.1) | collective-permute-done | bytes 237600 | tf_op jit(solution)/shard_map/ppermute | solution.py:43
  27.3 8.2 %collective-permute-done.2 = bf16[32,3712]{1,0:T(8,128)(2,1)S(1)} collective-permute-done((bf16[32,3712]{1,0:T(8,128)(2,1)S(1)}, bf16[32,3712]{1,0:T(8,128)(2,1)S(1)}, u32[]{:S(2)}, u32[]{:S(2)}) %collective-permute-start.2) | collective-permute-done | bytes 237600 | tf_op jit(solution)/shard_map/ppermute | solution.py:43
  35.6 8.2 %collective-permute-done.3 = bf16[32,3712]{1,0:T(8,128)(2,1)S(1)} collective-permute-done((bf16[32,3712]{1,0:T(8,128)(2,1)S(1)}, bf16[32,3712]{1,0:T(8,128)(2,1)S(1)}, u32[]{:S(2)}, u32[]{:S(2)}) %collective-permute-start.3) | collective-permute-done | bytes 237600 | tf_op jit(solution)/shard_map/ppermute | solution.py:43
  43.8 8.2 %collective-permute-done.4 = bf16[32,3712]{1,0:T(8,128)(2,1)S(1)} collective-permute-done((bf16[32,3712]{1,0:T(8,128)(2,1)S(1)}, bf16[32,3712]{1,0:T(8,128)(2,1)S(1)}, u32[]{:S(2)}, u32[]{:S(2)}) %collective-permute-start.4) | collective-permute-done | bytes 237600 | tf_op jit(solution)/shard_map/ppermute | solution.py:43
  52.0 8.2 %collective-permute-done.5 = bf16[32,3712]{1,0:T(8,128)(2,1)S(1)} collective-permute-done((bf16[32,3712]{1,0:T(8,128)(2,1)S(1)}, bf16[32,3712]{1,0:T(8,128)(2,1)S(1)}, u32[]{:S(2)}, u32[]{:S(2)}) %collective-permute-start.5) | collective-permute-done | bytes 237600 | tf_op jit(solution)/shard_map/ppermute | solution.py:43
  61.0 8.2 %collective-permute-done.6 = bf16[32,3712]{1,0:T(8,128)(2,1)S(1)} collective-permute-done((bf16[32,3712]{1,0:T(8,128)(2,1)S(1)}, bf16[32,3712]{1,0:T(8,128)(2,1)S(1)}, u32[]{:S(2)}, u32[]{:S(2)}) %collective-permute-start.6) | collective-permute-done | bytes 237600 | tf_op jit(solution)/shard_map/ppermute | solution.py:43
  69.9 8.2 %collective-permute-done.7 = bf16[32,3712]{1,0:T(8,128)(2,1)S(1)} collective-permute-done((bf16[32,3712]{1,0:T(8,128)(2,1)S(1)}, bf16[32,3712]{1,0:T(8,128)(2,1)S(1)}, u32[]{:S(2)}, u32[]{:S(2)}) %collective-permute-start.7) | collective-permute-done | bytes 237600 | tf_op jit(solution)/shard_map/ppermute | solution.py:43
  78.8 8.2 %collective-permute-done.8 = bf16[32,3712]{1,0:T(8,128)(2,1)S(1)} collective-permute-done((bf16[32,3712]{1,0:T(8,128)(2,1)S(1)}, bf16[32,3712]{1,0:T(8,128)(2,1)S(1)}, u32[]{:S(2)}, u32[]{:S(2)}) %collective-permute-start.8) | collective-permute-done | bytes 237600 | tf_op jit(solution)/shard_map/ppermute | solution.py:43
  87.7 8.2 %collective-permute-done.9 = bf16[32,3712]{1,0:T(8,128)(2,1)S(1)} collective-permute-done((bf16[32,3712]{1,0:T(8,128)(2,1)S(1)}, bf16[32,3712]{1,0:T(8,128)(2,1)S(1)}, u32[]{:S(2)}, u32[]{:S(2)}) %collective-permute-start.9) | collective-permute-done | bytes 237600 | tf_op jit(solution)/shard_map/ppermute | solution.py:43
  96.7 8.2 %collective-permute-done.10 = bf16[32,3712]{1,0:T(8,128)(2,1)S(1)} collective-permute-done((bf16[32,3712]{1,0:T(8,128)(2,1)S(1)}, bf16[32,3712]{1,0:T(8,128)(2,1)S(1)}, u32[]{:S(2)}, u32[]{:S(2)}) %collective-permute-start.10) | collective-permute-done | bytes 237600 | tf_op jit(solution)/shard_map/ppermute | solution.py:43
  105.6 8.2 %collective-permute-done.11 = bf16[32,3712]{1,0:T(8,128)(2,1)S(1)} collective-permute-done((bf16[32,3712]{1,0:T(8,128)(2,1)S(1)}, bf16[32,3712]{1,0:T(8,128)(2,1)S(1)}, u32[]{:S(2)}, u32[]{:S(2)}) %collective-permute-start.11) | collective-permute-done | bytes 237600 | tf_op jit(solution)/shard_map/ppermute | solution.py:43
  114.5 8.2 %collective-permute-done.12 = bf16[32,3712]{1,0:T(8,128)(2,1)S(1)} collective-permute-done((bf16[32,3712]{1,0:T(8,128)(2,1)S(1)}, bf16[32,3712]{1,0:T(8,128)(2,1)S(1)}, u32[]{:S(2)}, u32[]{:S(2)}) %collective-permute-start.12) | collective-permute-done | bytes 237600 | tf_op jit(solution)/shard_map/ppermute | solution.py:43
  123.4 8.3 %collective-permute-done.13 = bf16[32,3712]{1,0:T(8,128)(2,1)} collective-permute-done((bf16[32,3712]{1,0:T(8,128)(2,1)S(1)}, bf16[32,3712]{1,0:T(8,128)(2,1)}, u32[]{:S(2)}, u32[]{:S(2)}) %collective-permute-start.13) | collective-permute-done | bytes 237600 | tf_op jit(solution)/shard_map/ppermute | solution.py:43
  132.7 2.4 copy.103
  135.1 2.3 copy.102
  140.9 2.3 copy.99
  143.2 2.3 copy.98
  149.0 2.2 copy.95
  151.3 2.2 copy.94
  160.2 33.6 %concatenate.10 = bf16[1024,3712]{0,1:T(8,128)(2,1)} concatenate(bf16[32,3712]{0,1:T(8,128)(2,1)} %copy.91, bf16[32,3712]{0,1:T(8,128)(2,1)} %copy.92, bf16[32,3712]{0,1:T(8,128)(2,1)} %copy.93, bf16[32,3712]{0,1:T(8,128)(2,1)} %copy.94, bf16[32,3712]{0,1:T(8,128)(2,1)} %copy.95, bf16[32,3712]{0,1:T(8,128)(2,1)} %copy.96, bf16[32,3712]{0,1:T(8,128)(2,1)} %copy.97, ...), dimensions={0} | concatenate | bytes 15204352 | tf_op jit(solution)/shard_map/jit(_roll_dynamic)/concatenate | solution.py:44
  193.8 6.1 %fusion.2 = f32[512,512]{1,0:T(8,128)S(1)} fusion(bf16[1,3584,512]{2,1,0:T(8,128)(2,1)} %param.13, bf16[1024,3712]{0,1:T(8,128)(2,1)} %concatenate.10, s32[]{:T(128)S(6)} %select_n.34), kind=kOutput, calls=%fused_computation.3 | convolution fusion | flops 1879048192 | bytes 8388612 | tf_op jit(solution)/shard_map/dot_general | solution.py:53
  200.9 13.2 %convolution_multiply_fusion = f32[512,3584]{1,0:T(8,128)} fusion(bf16[1,512,3584]{2,1,0:T(8,128)(2,1)} %param.14, f32[512]{0:T(512)S(1)} %fusion.19, f32[512,512]{1,0:T(8,128)S(1)} %fusion.2, bf16[1,3584,512]{2,1,0:T(8,128)(2,1)} %param.12, bf16[1024,3712]{0,1:T(8,128)(2,1)} %concatenate.10, s32[]{:T(128)S(6)} %select_n.34), kind=kOutput, calls=%fused_computation.1 | convolution fusion | flops 3761504256 | bytes 19400708 | tf_op jit(solution)/shard_map/dot_general | solution.py:55
  217.0 90.1 %reduce-scatter.2.cloned.1.call-done = f32[32,3584]{1,0:T(8,128)} async-done(((f32[512,3584]{1,0:T(8,128)}), f32[32,3584]{1,0:T(8,128)}) %reduce-scatter.2.cloned.1.call-update) | async-done | bytes 458768 | tf_op jit(solution)/shard_map/reduce_scatter | solution.py:57
  (75 shorter events, 28.8 us)
Async XLA Ops:
  7.2 207.7 %copy-start = (bf16[4,64,576]{2,1,0:T(8,128)(2,1)S(1)}, bf16[4,64,576]{2,1,0:T(8,128)(2,1)}, u32[]{:S(2)}) copy-start(bf16[4,64,576]{2,1,0:T(8,128)(2,1)} %param.15) | copy-start | bytes 884740
  7.2 299.9 %reduce-scatter.2.cloned.1.call-start = ((), (), s32[]{:S(2)}) async-start(), calls=%async_computation.1 | async-start | bytes 7798784 | tf_op jit(solution)/shard_map/reduce_scatter | solution.py:57
  9.8 9.3 %collective-permute-start = (bf16[32,3712]{1,0:T(8,128)(2,1)S(1)}, bf16[32,3712]{1,0:T(8,128)(2,1)S(1)}, u32[]{:S(2)}, u32[]{:S(2)}) collective-permute-start(bf16[32,3712]{1,0:T(8,128)(2,1)S(1)} %copy.90), channel_id=1, source_target_pairs={{0,2},{2,4},{4,6},{6,8},{8,10},{10,12},{12,14},{14,16},{16,18},{18... | collective-permute-start | bytes 712712 | tf_op jit(solution)/shard_map/ppermute | solution.py:43
  19.1 8.2 %collective-permute-start.1 = (bf16[32,3712]{1,0:T(8,128)(2,1)S(1)}, bf16[32,3712]{1,0:T(8,128)(2,1)S(1)}, u32[]{:S(2)}, u32[]{:S(2)}) collective-permute-start(bf16[32,3712]{1,0:T(8,128)(2,1)S(1)} %collective-permute-done), channel_id=1, source_target_pairs={{0,2},{2,4},{4,6},{6,8},{8,10},{10,12},{12,14},{14,16},{16,18},{18... | collective-permute-start | bytes 712712 | tf_op jit(solution)/shard_map/ppermute | solution.py:43
  27.3 8.2 %collective-permute-start.2 = (bf16[32,3712]{1,0:T(8,128)(2,1)S(1)}, bf16[32,3712]{1,0:T(8,128)(2,1)S(1)}, u32[]{:S(2)}, u32[]{:S(2)}) collective-permute-start(bf16[32,3712]{1,0:T(8,128)(2,1)S(1)} %collective-permute-done.1), channel_id=1, source_target_pairs={{0,2},{2,4},{4,6},{6,8},{8,10},{10,12},{12,14},{14,16},{16,18},{18... | collective-permute-start | bytes 712712 | tf_op jit(solution)/shard_map/ppermute | solution.py:43
  35.6 96.2 %copy-start.2 = (bf16[32,3712]{1,0:T(8,128)(2,1)}, bf16[32,3712]{1,0:T(8,128)(2,1)S(1)}, u32[]{:S(2)}) copy-start(bf16[32,3712]{1,0:T(8,128)(2,1)S(1)} %collective-permute-done.2) | copy-start | bytes 712708
  35.6 8.2 %collective-permute-start.3 = (bf16[32,3712]{1,0:T(8,128)(2,1)S(1)}, bf16[32,3712]{1,0:T(8,128)(2,1)S(1)}, u32[]{:S(2)}, u32[]{:S(2)}) collective-permute-start(bf16[32,3712]{1,0:T(8,128)(2,1)S(1)} %collective-permute-done.2), channel_id=1, source_target_pairs={{0,2},{2,4},{4,6},{6,8},{8,10},{10,12},{12,14},{14,16},{16,18},{18... | collective-permute-start | bytes 712712 | tf_op jit(solution)/shard_map/ppermute | solution.py:43
  43.8 88.0 %copy-start.3 = (bf16[32,3712]{1,0:T(8,128)(2,1)}, bf16[32,3712]{1,0:T(8,128)(2,1)S(1)}, u32[]{:S(2)}) copy-start(bf16[32,3712]{1,0:T(8,128)(2,1)S(1)} %collective-permute-done.3) | copy-start | bytes 712708
  43.8 8.2 %collective-permute-start.4 = (bf16[32,3712]{1,0:T(8,128)(2,1)S(1)}, bf16[32,3712]{1,0:T(8,128)(2,1)S(1)}, u32[]{:S(2)}, u32[]{:S(2)}) collective-permute-start(bf16[32,3712]{1,0:T(8,128)(2,1)S(1)} %collective-permute-done.3), channel_id=1, source_target_pairs={{0,2},{2,4},{4,6},{6,8},{8,10},{10,12},{12,14},{14,16},{16,18},{18... | collective-permute-start | bytes 712712 | tf_op jit(solution)/shard_map/ppermute | solution.py:43
  52.0 79.8 %copy-start.4 = (bf16[32,3712]{1,0:T(8,128)(2,1)}, bf16[32,3712]{1,0:T(8,128)(2,1)S(1)}, u32[]{:S(2)}) copy-start(bf16[32,3712]{1,0:T(8,128)(2,1)S(1)} %collective-permute-done.4) | copy-start | bytes 712708
  52.0 8.2 %collective-permute-start.5 = (bf16[32,3712]{1,0:T(8,128)(2,1)S(1)}, bf16[32,3712]{1,0:T(8,128)(2,1)S(1)}, u32[]{:S(2)}, u32[]{:S(2)}) collective-permute-start(bf16[32,3712]{1,0:T(8,128)(2,1)S(1)} %collective-permute-done.4), channel_id=1, source_target_pairs={{0,2},{2,4},{4,6},{6,8},{8,10},{10,12},{12,14},{14,16},{16,18},{18... | collective-permute-start | bytes 712712 | tf_op jit(solution)/shard_map/ppermute | solution.py:43
  61.0 8.2 %collective-permute-start.6 = (bf16[32,3712]{1,0:T(8,128)(2,1)S(1)}, bf16[32,3712]{1,0:T(8,128)(2,1)S(1)}, u32[]{:S(2)}, u32[]{:S(2)}) collective-permute-start(bf16[32,3712]{1,0:T(8,128)(2,1)S(1)} %collective-permute-done.5), channel_id=1, source_target_pairs={{0,2},{2,4},{4,6},{6,8},{8,10},{10,12},{12,14},{14,16},{16,18},{18... | collective-permute-start | bytes 712712 | tf_op jit(solution)/shard_map/ppermute | solution.py:43
  69.9 8.2 %collective-permute-start.7 = (bf16[32,3712]{1,0:T(8,128)(2,1)S(1)}, bf16[32,3712]{1,0:T(8,128)(2,1)S(1)}, u32[]{:S(2)}, u32[]{:S(2)}) collective-permute-start(bf16[32,3712]{1,0:T(8,128)(2,1)S(1)} %collective-permute-done.6), channel_id=1, source_target_pairs={{0,2},{2,4},{4,6},{6,8},{8,10},{10,12},{12,14},{14,16},{16,18},{18... | collective-permute-start | bytes 712712 | tf_op jit(solution)/shard_map/ppermute | solution.py:43
  78.8 8.2 %collective-permute-start.8 = (bf16[32,3712]{1,0:T(8,128)(2,1)S(1)}, bf16[32,3712]{1,0:T(8,128)(2,1)S(1)}, u32[]{:S(2)}, u32[]{:S(2)}) collective-permute-start(bf16[32,3712]{1,0:T(8,128)(2,1)S(1)} %collective-permute-done.7), channel_id=1, source_target_pairs={{0,2},{2,4},{4,6},{6,8},{8,10},{10,12},{12,14},{14,16},{16,18},{18... | collective-permute-start | bytes 712712 | tf_op jit(solution)/shard_map/ppermute | solution.py:43
  87.7 8.2 %collective-permute-start.9 = (bf16[32,3712]{1,0:T(8,128)(2,1)S(1)}, bf16[32,3712]{1,0:T(8,128)(2,1)S(1)}, u32[]{:S(2)}, u32[]{:S(2)}) collective-permute-start(bf16[32,3712]{1,0:T(8,128)(2,1)S(1)} %collective-permute-done.8), channel_id=1, source_target_pairs={{0,2},{2,4},{4,6},{6,8},{8,10},{10,12},{12,14},{14,16},{16,18},{18... | collective-permute-start | bytes 712712 | tf_op jit(solution)/shard_map/ppermute | solution.py:43
  96.6 8.2 %collective-permute-start.10 = (bf16[32,3712]{1,0:T(8,128)(2,1)S(1)}, bf16[32,3712]{1,0:T(8,128)(2,1)S(1)}, u32[]{:S(2)}, u32[]{:S(2)}) collective-permute-start(bf16[32,3712]{1,0:T(8,128)(2,1)S(1)} %collective-permute-done.9), channel_id=1, source_target_pairs={{0,2},{2,4},{4,6},{6,8},{8,10},{10,12},{12,14},{14,16},{16,18},{18... | collective-permute-start | bytes 712712 | tf_op jit(solution)/shard_map/ppermute | solution.py:43
  104.9 0.7 copy-start.12
  105.6 8.2 %collective-permute-start.11 = (bf16[32,3712]{1,0:T(8,128)(2,1)S(1)}, bf16[32,3712]{1,0:T(8,128)(2,1)S(1)}, u32[]{:S(2)}, u32[]{:S(2)}) collective-permute-start(bf16[32,3712]{1,0:T(8,128)(2,1)S(1)} %collective-permute-done.10), channel_id=1, source_target_pairs={{0,2},{2,4},{4,6},{6,8},{8,10},{10,12},{12,14},{14,16},{16,18},{18... | collective-permute-start | bytes 712712 | tf_op jit(solution)/shard_map/ppermute | solution.py:43
  114.5 8.2 %collective-permute-start.12 = (bf16[32,3712]{1,0:T(8,128)(2,1)S(1)}, bf16[32,3712]{1,0:T(8,128)(2,1)S(1)}, u32[]{:S(2)}, u32[]{:S(2)}) collective-permute-start(bf16[32,3712]{1,0:T(8,128)(2,1)S(1)} %collective-permute-done.11), channel_id=1, source_target_pairs={{0,2},{2,4},{4,6},{6,8},{8,10},{10,12},{12,14},{14,16},{16,18},{18... | collective-permute-start | bytes 712712 | tf_op jit(solution)/shard_map/ppermute | solution.py:43
  123.4 8.3 %collective-permute-start.13 = (bf16[32,3712]{1,0:T(8,128)(2,1)S(1)}, bf16[32,3712]{1,0:T(8,128)(2,1)}, u32[]{:S(2)}, u32[]{:S(2)}) collective-permute-start(bf16[32,3712]{1,0:T(8,128)(2,1)S(1)} %collective-permute-done.12), channel_id=1, source_target_pairs={{0,2},{2,4},{4,6},{6,8},{8,10},{10,12},{12,14},{14,16},{16,18},{18... | collective-permute-start | bytes 712712 | tf_op jit(solution)/shard_map/ppermute | solution.py:43
  131.8 26.2 %collective-permute-start.14 = (bf16[32,3712]{1,0:T(8,128)(2,1)}, bf16[32,3712]{1,0:T(8,128)(2,1)}, u32[]{:S(2)}, u32[]{:S(2)}) collective-permute-start(bf16[32,3712]{1,0:T(8,128)(2,1)} %collective-permute-done.13), channel_id=1, source_target_pairs={{0,2},{2,4},{4,6},{6,8},{8,10},{10,12},{12,14},{14,16},{16,18},{18... | collective-permute-start | bytes 712712 | tf_op jit(solution)/shard_map/ppermute | solution.py:43
  132.7 6.9 %copy-start.6 = (bf16[32,3712]{1,0:T(8,128)(2,1)S(1)}, bf16[32,3712]{1,0:T(8,128)(2,1)}, u32[]{:S(2)}) copy-start(bf16[32,3712]{1,0:T(8,128)(2,1)} %copy-done.5) | copy-start | bytes 712708
  140.9 6.8 %copy-start.11 = (bf16[32,3712]{1,0:T(8,128)(2,1)S(1)}, bf16[32,3712]{1,0:T(8,128)(2,1)}, u32[]{:S(2)}) copy-start(bf16[32,3712]{1,0:T(8,128)(2,1)} %copy-done.10) | copy-start | bytes 712708
  214.2 1.1 copy-start.1
  (8 other events, 5.5 us)
Sparse Core Ops, SparseCore 0:
  214.3 92.7 reduce-scatter.1
